TPU v7x, 512 devices: a whole 4x8x8 slice. The times are simulated.
512 devices in a mesh: segment: 4 (over z_lo), seq: 16 (over z_hi, x, core), mp: 8 (over y).
Axes of the slice: x: 4, y: 8, z: 8 (z_hi: 2, z_lo: 4; z = z_hi * 4 + z_lo), core: 2. Of those that a mesh axis runs over, the one named last changes fastest.
Arguments:
- latents: bfloat16 [4, 16, 256, 4096], P('segment', 'seq', None, 'mp'), may hold values from -6 to 6
- w_qkv: bfloat16 [4, 4096, 3, 4096], P('segment', 'seq', None, 'mp'), may hold values from -1 to 1
- w_out: bfloat16 [4, 4096, 4096], P('segment', 'mp', 'seq'), may hold values from -0.09375 to 0.09375
- mod_shift: float32 [4, 4096], P('segment'), may hold values from -3 to 3
- mod_scale: float32 [4, 4096], P('segment'), may hold values from 0.1 to 1.9
- mod_gate: float32 [4, 4096], P('segment'), may hold values from 0.5 to 1.5
- counts: int32 [4, 16], P('segment'), may hold values from 64 to 256, as said below
Outputs:
- next_latents: bfloat16 [4, 16, 256, 4096], P('segment', 'seq', None, 'mp')
Inputs may be any that keep to these rules, and one draw needn't show every extreme that they name: `counts`: in every section's clip at least one frame has all 256 patch positions valid.
All inputs are finite; a program needn't handle non-finite values.
Results may differ from a plain program's by a relative error of at most 0.01.
Values may be sent and summed in bfloat16 or wider, within the bound.
No kernel may reach another device: no remote copies, remote signals or barrier semaphores. Data moves between devices by JAX's collectives and lax.ppermute only.
A program may use at most 64 MiB of HBM per device.

v0:
```python
import math
import jax
import jax.numpy as jnp
from jax import lax
from jax.sharding import PartitionSpec as P

HD = 128
EPS = 1e-06
NEG_FILL = -1e30


def passed_along(x, axis, by):
    length = lax.axis_size(axis)
    return lax.ppermute(x, axis, [(i, (i + by) % length) for i in range(length)])


def masked_attention(queries, keys_in, values, usable):
    factor = 1.0 / math.sqrt(queries.shape[-1])
    scores = (
        jnp.einsum("...ihe,...jhe->...hij", queries, keys_in, preferred_element_type=jnp.float32)
        * factor
    )
    allowed = usable[..., None, :, None] & usable[..., None, None, :]
    masked = jnp.where(allowed, scores, NEG_FILL)
    highest = jnp.max(masked, axis=-1, keepdims=True)
    raised = jnp.where(allowed, jnp.exp(masked - highest), 0.0)
    spare_one = jnp.where(usable, 0.0, 1.0)[..., None, :, None]
    weights = (raised / (jnp.sum(raised, axis=-1, keepdims=True) + spare_one)).astype(jnp.bfloat16)
    blended = jnp.einsum(
        "...hij,...jhe->...ihe", weights, values, preferred_element_type=jnp.float32
    )
    return blended.astype(jnp.bfloat16)


def relay_features(rows_now):
    return lax.all_to_all(rows_now, "seq", split_axis=0, concat_axis=0, tiled=True)


def pass_onward(rows_now):
    return passed_along(rows_now, "segment", 1)


def on_device(latents, w_qkv, w_out, mod_shift, mod_scale, mod_gate, counts):
    frames = lax.axis_size("seq")
    patches = latents.shape[2]
    narrow = latents.shape[3]
    span = patches // frames
    segment_rows = latents[0, 0]
    gathered = lax.all_gather(latents, "mp", axis=3, tiled=True)[0, 0]
    widened = gathered.astype(jnp.float32)
    average = jnp.mean(widened, axis=-1, keepdims=True)
    centred = widened - average
    variance = jnp.mean(centred * centred, axis=-1, keepdims=True)
    modulated = (centred * lax.rsqrt(variance + EPS) * mod_scale[0] + mod_shift[0]).astype(
        jnp.bfloat16
    )
    columns = w_qkv.shape[2] * w_qkv.shape[3]
    piece = lax.all_gather(w_qkv, "seq", axis=1, tiled=True)
    height = piece.shape[1]
    projected = jnp.dot(
        modulated, piece.reshape(height, columns), preferred_element_type=jnp.float32
    )
    local_heads = w_qkv.shape[3] // HD
    projected = projected.astype(jnp.bfloat16).reshape(patches, 3, local_heads, HD)
    frame_here = lax.axis_index("seq")
    clip_counts = counts[0]
    positions = jnp.arange(frames)

    def spatial(triple):
        count_here = jnp.sum(jnp.where(positions == frame_here, clip_counts, 0))
        usable = jnp.arange(patches) < count_here
        return masked_attention(triple[:, 0], triple[:, 1], triple[:, 2], usable)

    def temporal(triple):
        by_place = triple.reshape(frames, span, 3, local_heads, HD).transpose(1, 0, 2, 3, 4)
        location = frame_here * span + jnp.arange(span)
        usable = location[:, None] < clip_counts[None, :]
        blended = masked_attention(by_place[:, :, 0], by_place[:, :, 1], by_place[:, :, 2], usable)
        return blended.transpose(1, 0, 2, 3).reshape(patches, local_heads, HD)

    attended = lax.cond(lax.axis_index("segment") % 2 == 0, spatial, temporal, projected)
    attended = attended.reshape(patches, local_heads * HD)
    out_whole = lax.all_gather(w_out, "seq", axis=2, tiled=True)[0]
    member = lax.axis_index("mp")
    partials = jnp.dot(attended, out_whole, preferred_element_type=jnp.float32)
    summed = lax.psum_scatter(
        partials.astype(jnp.bfloat16), "mp", scatter_dimension=1, tiled=True
    ).astype(jnp.float32)
    gate_here = lax.dynamic_slice_in_dim(mod_gate[0], member * narrow, narrow)
    updated = (segment_rows.astype(jnp.float32) + gate_here * summed).astype(jnp.bfloat16)
    updated = updated.reshape(frames, span, narrow)
    moved = pass_onward(relay_features(updated))
    return moved.reshape(1, 1, patches, narrow)


def solution(mesh):
    return jax.shard_map(
        on_device,
        mesh=mesh,
        in_specs=(
            P("segment", "seq", None, "mp"),
            P("segment", "seq", None, "mp"),
            P("segment", "mp", "seq"),
            P("segment", None),
            P("segment", None),
            P("segment", None),
            P("segment", None),
        ),
        out_specs=P("segment", "seq", None, "mp"),
        check_vma=False,
    )
```

profile of v0, /device:TPU:1, one launch (start us, length us, event | category | flops | bytes accessed | tf_op | source)
XLA Modules:
  0.0 384.6 jit_solution(8186895898152812026)
XLA Ops:
  6.5 0.7 all-gather.4.cloned.1.call-update
  7.3 2.3 copy.18
  9.7 0.7 all-gather.8.cloned.1.call-update
  10.5 43.7 %all-gather.4.cloned.1.call-done = bf16[1,1,256,4096]{3,2,1,0:T(8,128)(2,1)} async-done(((bf16[1,1,256,512]{3,2,1,0:T(8,128)(2,1)}), bf16[1,1,256,4096]{3,2,1,0:T(8,128)(2,1)}) %all-gather.4.cloned.1.call-update) | async-done | bytes 2097168 | tf_op jit(solution)/shard_map/all_gather | solution.py:49
  54.1 2.1 convert_reduce_fusion
  56.2 2.3 fusion.30
  58.5 157.1 %all-gather.6.cloned.1.call-done = bf16[1,4096,3,512]{1,3,2,0:T(8,128)(2,1)} async-done(((bf16[1,256,3,512]{1,3,2,0:T(8,128)(2,1)}), bf16[1,4096,3,512]{1,3,2,0:T(8,128)(2,1)}) %all-gather.6.cloned.1.call-update) | async-done | bytes 12582928 | tf_op jit(solution)/shard_map/all_gather | solution.py:58
  215.7 8.2 %convolution_convert_fusion.3 = bf16[256,1536]{1,0:T(8,128)(2,1)S(1)} fusion(bf16[4096,1536]{0,1:T(8,128)(2,1)} %bitcast.96, bf16[1,1,256,4096]{3,2,1,0:T(8,128)(2,1)S(1)} %copy-done.1, f32[4096]{0:T(1024)S(1)} %bitcast.97, f32[4096]{0:T(1024)S(1)} %bitcast.98, f32[256]{0:T(256)S(1)} %add_rsqrt_fusion, f32[256]{0:T(256)S(1)} %broadcast_multiply_fusion), kind=kOutput, calls=%fused_computation.58 | convolution fusion | flops 3227910144 | bytes 15501312 | tf_op jit(solution)/shard_map/dot_general | solution.py:60
  223.9 3.7 conditional.1
  223.9 0.6 fusion.14
  224.6 0.6 iota_compare_fusion
  225.1 0.1 broadcast_and_fusion.1
  225.2 0.3 copy.19
  225.5 0.6 fusion.40
  226.2 0.6 broadcast_select_fusion.1
  226.7 0.8 convolution_convert_fusion.1
  227.6 71.0 %all-gather.8.cloned.1.call-done = bf16[1,512,4096]{2,1,0:T(8,128)(2,1)} async-done(((bf16[1,512,256]{2,1,0:T(8,128)(2,1)}), bf16[1,512,4096]{2,1,0:T(8,128)(2,1)}) %all-gather.8.cloned.1.call-update) | async-done | bytes 4194320 | tf_op jit(solution)/shard_map/all_gather | solution.py:83
  298.5 4.8 %convolution_convert_fusion.2 = bf16[256,4096]{1,0:T(8,128)(2,1)} fusion(bf16[256,512]{0,1:T(8,128)(2,1)S(1)} %get-tuple-element.36, bf16[1,512,4096]{2,1,0:T(8,128)(2,1)} %all-gather.8.cloned.1.call-done), kind=kOutput, calls=%fused_computation.49 | convolution fusion | flops 1074790400 | bytes 6553600 | tf_op jit(solution)/shard_map/dot_general | solution.py:85
  303.4 36.3 %reduce-scatter.2.cloned.1.call-done = bf16[256,512]{1,0:T(8,128)(2,1)} async-done(((bf16[256,4096]{1,0:T(8,128)(2,1)}), bf16[256,512]{1,0:T(8,128)(2,1)}) %reduce-scatter.2.cloned.1.call-update) | async-done | bytes 262160 | tf_op jit(solution)/shard_map/reduce_scatter | solution.py:86
  339.7 1.0 fusion.38
  340.7 26.0 %all_to_all.5 = bf16[16,16,512]{2,1,0:T(8,128)(2,1)S(1)} all-to-all(bf16[16,16,512]{2,1,0:T(8,128)(2,1)S(1)} %bitcast.84), channel_id=1, replica_groups=mesh['segment'=4,'seq'=16,'mp'=8] {'seq'}, dimensions={0} | all-to-all | bytes 524288 | tf_op jit(solution)/shard_map/all_to_all | solution.py:36
  366.8 5.0 %collective-permute-start = (bf16[16,16,512]{2,1,0:T(8,128)(2,1)S(1)}, bf16[16,16,512]{2,1,0:T(8,128)(2,1)S(1)}, u32[]{:S(2)}, u32[]{:S(2)}) collective-permute-start(bf16[16,16,512]{2,1,0:T(8,128)(2,1)S(1)} %all_to_all.5), channel_id=1, source_target_pairs={{0,128},{128,256},{256,384},{384,0},{1,129},{129,257},{257,385},{3... | collective-permute-start | bytes 786440 | tf_op jit(solution)/shard_map/ppermute | solution.py:14
  371.7 5.6 %collective-permute-done = bf16[16,16,512]{2,1,0:T(8,128)(2,1)S(1)} collective-permute-done((bf16[16,16,512]{2,1,0:T(8,128)(2,1)S(1)}, bf16[16,16,512]{2,1,0:T(8,128)(2,1)S(1)}, u32[]{:S(2)}, u32[]{:S(2)}) %collective-permute-start) | collective-permute-done | bytes 262176 | tf_op jit(solution)/shard_map/ppermute | solution.py:14
  377.4 0.7 copy.32
  (23 shorter events, 0.2 us)
Async XLA Ops:
  6.5 296.9 %copy-start = (f32[1,4096]{1,0:T(1,128)S(1)}, f32[1,4096]{1,0:T(1,128)}, u32[]{:S(2)}) copy-start(f32[1,4096]{1,0:T(1,128)} %param.14) | copy-start | bytes 49156
  6.5 209.1 %copy-start.5 = (f32[1,4096]{1,0:T(1,128)S(1)}, f32[1,4096]{1,0:T(1,128)}, u32[]{:S(2)}) copy-start(f32[1,4096]{1,0:T(1,128)} %param.13) | copy-start | bytes 49156
  6.5 209.1 %copy-start.4 = (f32[1,4096]{1,0:T(1,128)S(1)}, f32[1,4096]{1,0:T(1,128)}, u32[]{:S(2)}) copy-start(f32[1,4096]{1,0:T(1,128)} %param.12) | copy-start | bytes 49156
  6.5 47.6 %all-gather.4.cloned.1.call-start = ((), (), s32[]{:S(2)}) async-start(), calls=%async_computation.2 | async-start | bytes 2359296 | tf_op jit(solution)/shard_map/all_gather | solution.py:49
  7.3 208.4 %all-gather.6.cloned.1.call-start = ((), (), s32[]{:S(2)}) async-start(), calls=%async_computation.3 | async-start | bytes 13369344 | tf_op jit(solution)/shard_map/all_gather | solution.py:58
  9.7 288.9 %all-gather.8.cloned.1.call-start = ((), (), s32[]{:S(2)}) async-start(), calls=%async_computation.4 | async-start | bytes 4456448 | tf_op jit(solution)/shard_map/all_gather | solution.py:83
  10.4 329.3 %reduce-scatter.2.cloned.1.call-start = ((), (), s32[]{:S(2)}) async-start(), calls=%async_computation.5 | async-start | bytes 2359296 | tf_op jit(solution)/shard_map/reduce_scatter | solution.py:86
  54.1 161.5 %copy-start.1 = (bf16[1,1,256,4096]{3,2,1,0:T(8,128)(2,1)S(1)}, bf16[1,1,256,4096]{3,2,1,0:T(8,128)(2,1)}, u32[]{:S(2)}) copy-start(bf16[1,1,256,4096]{3,2,1,0:T(8,128)(2,1)} %all-gather.4.cloned.1.call-done) | copy-start | bytes 6291460
  215.7 8.3 %copy-start.3 = (s32[1,16]{1,0:T(1,128)S(1)}, s32[1,16]{1,0:T(1,128)}, u32[]{:S(2)}) copy-start(s32[1,16]{1,0:T(1,128)} %param.15) | copy-start | bytes 196
  227.6 112.1 %copy-start.2 = (bf16[1,1,256,512]{3,2,1,0:T(8,128)(2,1)S(1)}, bf16[1,1,256,512]{3,2,1,0:T(8,128)(2,1)}, u32[]{:S(2)}) copy-start(bf16[1,1,256,512]{3,2,1,0:T(8,128)(2,1)} %param.9) | copy-start | bytes 786436
  366.8 10.6 %collective-permute-start = (bf16[16,16,512]{2,1,0:T(8,128)(2,1)S(1)}, bf16[16,16,512]{2,1,0:T(8,128)(2,1)S(1)}, u32[]{:S(2)}, u32[]{:S(2)}) collective-permute-start(bf16[16,16,512]{2,1,0:T(8,128)(2,1)S(1)} %all_to_all.5), channel_id=1, source_target_pairs={{0,128},{128,256},{256,384},{384,0},{1,129},{129,257},{257,385},{3... | collective-permute-start | bytes 786440 | tf_op jit(solution)/shard_map/ppermute | solution.py:14
Sparse Core Ops, SparseCore 0:
  9.4 44.6 all-gather.3
  57.3 158.3 all-gather.5
  218.8 79.7 all-gather.7
  303.5 36.1 reduce-scatter.1
where the time goes:
time: 385 us
  waiting for transfers between devices  315 us (82%)
  blocking collectives  26 us (7%)
  matrix products  14.5 us (4%)
  between operations  13.2 us (3%)
  other arithmetic  7.29 us (2%)
  starting transfers between devices  5.07 us (1%)
    all_gather x1, waiting for transfers between devices, on_device(): piece = lax.all_gather(w_qkv, 'seq', axis=1, tiled=True)  157 us
    all_gather x1, waiting for transfers between devices, on_device(): out_whole = lax.all_gather(w_out, 'seq', axis=2, tiled=True)[0]  71 us
    all_gather x1, waiting for transfers between devices, on_device(): gathered = lax.all_gather(latents, 'mp', axis=3, tiled=True)[0, 0]  43.7 us
    reduce_scatter x1, waiting for transfers between devices, on_device(): lax.psum_scatter(partials.astype(jnp.bfloat16), 'mp', scatter_dimension=1...  36.3 us
    all_to_all x1, blocking collectives, relay_features(): lax.all_to_all(rows_now, 'seq', split_axis=0, concat_axis=0, tiled=True)  26 us
    dot_general x1, matrix products, on_device(): jnp.dot(modulated, piece.reshape(height, columns), preferred_element_type...  8.22 us
  transfers between devices with their start and end apart: 5, of which 5 were waited for; matrix products, arithmetic and copies ran while one was open for 5% of the time, Pallas kernels for 0%

commit v1 on v0

--- a/solution.py
+++ b/solution.py
@@ -7,6 +7,22 @@
 HD = 128
 EPS = 1e-06
 NEG_FILL = -1e30
+
+
+def ring_gather(x, axis, dim):
+    ways, here, step = (lax.axis_size(axis), lax.axis_index(axis), x.shape[dim])
+    lengths = [n * ways if d == dim else n for d, n in enumerate(x.shape)]
+    full = lax.dynamic_update_slice_in_dim(jnp.zeros(lengths, x.dtype), x, here * step, axis=dim)
+    going_up = going_down = x
+    for far in range(1, ways // 2 + 1):
+        going_up = lax.ppermute(going_up, axis, [(d, (d + 1) % ways) for d in range(ways)])
+        full = lax.dynamic_update_slice_in_dim(full, going_up, (here - far) % ways * step, axis=dim)
+        if 2 * far < ways:
+            going_down = lax.ppermute(going_down, axis, [(d, (d - 1) % ways) for d in range(ways)])
+            full = lax.dynamic_update_slice_in_dim(
+                full, going_down, (here + far) % ways * step, axis=dim
+            )
+    return full
 
 
 def passed_along(x, axis, by):
@@ -46,7 +62,7 @@
     narrow = latents.shape[3]
     span = patches // frames
     segment_rows = latents[0, 0]
-    gathered = lax.all_gather(latents, "mp", axis=3, tiled=True)[0, 0]
+    gathered = ring_gather(latents, "mp", 3)[0, 0]
     widened = gathered.astype(jnp.float32)
     average = jnp.mean(widened, axis=-1, keepdims=True)
     centred = widened - average

time: 385 us -> 341 us (0.89)
  waiting for transfers between devices: 315 us -> 250 us
  starting transfers between devices: 5.07 us -> 28.3 us
    all_gather x1 -> x0, waiting for transfers between devices: 43.7 us -> none  [on_device(): gathered = lax.all_gather(latents, 'mp', axis=3, tiled=True)[0, 0]]
    all_gather x1, waiting for transfers between devices: 157 us -> 122 us  [on_device(): piece = lax.all_gather(w_qkv, 'seq', axis=1, tiled=True)]
    ppermute x0 -> x7, starting transfers between devices: none -> 23.5 us  [the longest x3 13.1 us: ring_gather(): lax.ppermute(going_down, axis, [(d, (d - 1) % ways) for d in range(ways)])]
    ppermute x0 -> x7, waiting for transfers between devices: none -> 14.4 us  [the longest x4 14.4 us: ring_gather(): lax.ppermute(going_up, axis, [(d, (d + 1) % ways) for d in range(ways)])]
  transfers between devices with their start and end apart: 5 -> 11, of which waited for: 5 -> 8; matrix products, arithmetic and copies ran while one was open for 5% -> 4% of each run, Pallas kernels for 0% -> 0%
where the time goes in v1:
time: 341 us; the launch traced here: 340 us
  waiting for transfers between devices  250 us (73%)
  starting transfers between devices  28.3 us (8%)
  blocking collectives  26 us (8%)
  matrix products  14.3 us (4%)
  between operations  13.5 us (4%)
  other arithmetic  3.97 us (1%)
  local copies, waits for them, and re-layouts  3.79 us (1%)
    all_gather x1, waiting for transfers between devices, on_device(): piece = lax.all_gather(w_qkv, 'seq', axis=1, tiled=True)  122 us
    all_gather x1, waiting for transfers between devices, on_device(): out_whole = lax.all_gather(w_out, 'seq', axis=2, tiled=True)[0]  71.1 us
    reduce_scatter x1, waiting for transfers between devices, on_device(): lax.psum_scatter(partials.astype(jnp.bfloat16), 'mp', scatter_dimension=1...  36.3 us
    all_to_all x1, blocking collectives, relay_features(): lax.all_to_all(rows_now, 'seq', split_axis=0, concat_axis=0, tiled=True)  26 us
    ppermute x4, waiting for transfers between devices, ring_gather(): lax.ppermute(going_up, axis, [(d, (d + 1) % ways) for d in range(ways)])  14.4 us
    ppermute x3, starting transfers between devices, ring_gather(): lax.ppermute(going_down, axis, [(d, (d - 1) % ways) for d in range(ways)])  13.1 us
    ppermute x4, starting transfers between devices, ring_gather(): lax.ppermute(going_up, axis, [(d, (d + 1) % ways) for d in range(ways)])  10.4 us
    dot_general x1, matrix products, on_device(): jnp.dot(modulated, piece.reshape(height, columns), preferred_element_type...  8.06 us
  transfers between devices with their start and end apart: 11, of which 8 were waited for; matrix products, arithmetic and copies ran while one was open for 4% of the time, Pallas kernels for 0%

profile of v1, /device:TPU:1, one launch (start us, length us, event | category | flops | bytes accessed | tf_op | source)
XLA Modules:
  0.0 340.3 jit_solution(15700937758997261299)
XLA Ops:
  6.5 2.3 copy.18
  9.7 4.0 %collective-permute-start = (bf16[1,1,256,512]{3,2,1,0:T(8,128)(2,1)S(1)}, bf16[1,1,256,512]{3,2,1,0:T(8,128)(2,1)S(1)}, u32[]{:S(2)}, u32[]{:S(2)}) collective-permute-start(bf16[1,1,256,512]{3,2,1,0:T(8,128)(2,1)S(1)} %copy-done.1), channel_id=1, source_target_pairs={{0,1},{1,2},{2,3},{3,4},{4,5},{5,6},{6,7},{7,0},{8,9},{9,10},{10,1... | collective-permute-start | bytes 786440 | tf_op jit(solution)/shard_map/ppermute | solution.py:18
  13.7 3.8 %collective-permute-start.1 = (bf16[1,1,256,512]{3,2,1,0:T(8,128)(2,1)S(1)}, bf16[1,1,256,512]{3,2,1,0:T(8,128)(2,1)S(1)}, u32[]{:S(2)}, u32[]{:S(2)}) collective-permute-start(bf16[1,1,256,512]{3,2,1,0:T(8,128)(2,1)S(1)} %copy-done.1), channel_id=1, source_target_pairs={{0,7},{1,0},{2,1},{3,2},{4,3},{5,4},{6,5},{7,6},{8,15},{9,8},{10,9... | collective-permute-start | bytes 786440 | tf_op jit(solution)/shard_map/ppermute | solution.py:21
  18.0 1.4 collective-permute-done
  19.4 2.5 collective-permute-start.2
  21.9 4.7 %collective-permute-start.3 = (bf16[1,1,256,512]{3,2,1,0:T(8,128)(2,1)S(1)}, bf16[1,1,256,512]{3,2,1,0:T(8,128)(2,1)S(1)}, u32[]{:S(2)}, u32[]{:S(2)}) collective-permute-start(bf16[1,1,256,512]{3,2,1,0:T(8,128)(2,1)S(1)} %collective-permute-done.1), channel_id=1, source_target_pairs={{0,7},{1,0},{2,1},{3,2},{4,3},{5,4},{6,5},{7,6},{8,15},{9,8},{10,9... | collective-permute-start | bytes 786440 | tf_op jit(solution)/shard_map/ppermute | solution.py:21
  26.7 1.7 collective-permute-done.2
  28.4 1.9 collective-permute-start.4
  30.4 4.6 %collective-permute-start.5 = (bf16[1,1,256,512]{3,2,1,0:T(8,128)(2,1)S(1)}, bf16[1,1,256,512]{3,2,1,0:T(8,128)(2,1)S(1)}, u32[]{:S(2)}, u32[]{:S(2)}) collective-permute-start(bf16[1,1,256,512]{3,2,1,0:T(8,128)(2,1)S(1)} %collective-permute-done.3), channel_id=1, source_target_pairs={{0,7},{1,0},{2,1},{3,2},{4,3},{5,4},{6,5},{7,6},{8,15},{9,8},{10,9... | collective-permute-start | bytes 786440 | tf_op jit(solution)/shard_map/ppermute | solution.py:21
  35.0 3.0 collective-permute-done.4
  38.0 1.9 collective-permute-start.6
  40.0 8.3 %collective-permute-done.6 = bf16[1,1,256,512]{3,2,1,0:T(8,128)(2,1)S(1)} collective-permute-done((bf16[1,1,256,512]{3,2,1,0:T(8,128)(2,1)S(1)}, bf16[1,1,256,512]{3,2,1,0:T(8,128)(2,1)S(1)}, u32[]{:S(2)}, u32[]{:S(2)}) %collective-permute-start.6) | collective-permute-done | bytes 262176 | tf_op jit(solution)/shard_map/ppermute | solution.py:18
  49.4 122.0 %all-gather.3.cloned.1.call-done = bf16[1,4096,3,512]{1,3,2,0:T(8,128)(2,1)} async-done(((bf16[1,256,3,512]{1,3,2,0:T(8,128)(2,1)}), bf16[1,4096,3,512]{1,3,2,0:T(8,128)(2,1)}) %all-gather.3.cloned.1.call-update) | async-done | bytes 12582928 | tf_op jit(solution)/shard_map/all_gather | solution.py:74
  171.4 8.1 %convolution_convert_fusion.3 = bf16[256,1536]{1,0:T(8,128)(2,1)S(1)} fusion(bf16[4096,1536]{0,1:T(8,128)(2,1)} %bitcast.99, bf16[256,4096]{1,0:T(8,128)(2,1)S(1)} %bitcast_dynamic-update-slice_fusion, f32[4096]{0:T(1024)S(1)} %bitcast.100, f32[4096]{0:T(1024)S(1)} %bitcast.101, f32[256]{0:T(256)S(1)} %add_rsqrt_fusion, f32[256]{0:T(256)S(1)} %broadcast_multiply_fusion), kind=kOutput, calls=%fused_computation.56 | convolution fusion | flops 3227910144 | bytes 15501312 | tf_op jit(solution)/shard_map/dot_general | solution.py:76
  179.5 3.7 %conditional.1 = (bf16[256,512]{0,1:T(8,128)(2,1)S(1)}) conditional(s32[]{:T(128)} %convert_element_type.44, (s32[]{:T(128)}, s32[1,16]{1,0:T(1,128)S(1)}, bf16[256,1536]{1,0:T(8,128)(2,1)S(1)}) %tuple.24, (s32[]{:T(128)}, s32[16]{0:T(128)S(1)}, s32[1,16]{1,0:T(1,128)S(1)}, bf16[256,1536]{1,0:T(8,128)(2,1)S(1)}) %tuple.25), branch_computations={%region_2.5_spmd, %region_5.9_spmd} | conditional | flops 204410160 | bytes 6552408 | solution.py:97
  182.3 0.8 convolution_convert_fusion.1
  183.2 71.1 %all-gather.5.cloned.1.call-done = bf16[1,512,4096]{2,1,0:T(8,128)(2,1)} async-done(((bf16[1,512,256]{2,1,0:T(8,128)(2,1)}), bf16[1,512,4096]{2,1,0:T(8,128)(2,1)}) %all-gather.5.cloned.1.call-update) | async-done | bytes 4194320 | tf_op jit(solution)/shard_map/all_gather | solution.py:99
  254.3 4.8 %convolution_convert_fusion.2 = bf16[256,4096]{1,0:T(8,128)(2,1)} fusion(bf16[256,512]{0,1:T(8,128)(2,1)S(1)} %get-tuple-element.36, bf16[1,512,4096]{2,1,0:T(8,128)(2,1)} %all-gather.5.cloned.1.call-done), kind=kOutput, calls=%fused_computation.48 | convolution fusion | flops 1074790400 | bytes 6553600 | tf_op jit(solution)/shard_map/dot_general | solution.py:101
  259.2 36.3 %reduce-scatter.2.cloned.1.call-done = bf16[256,512]{1,0:T(8,128)(2,1)} async-done(((bf16[256,4096]{1,0:T(8,128)(2,1)}), bf16[256,512]{1,0:T(8,128)(2,1)}) %reduce-scatter.2.cloned.1.call-update) | async-done | bytes 262160 | tf_op jit(solution)/shard_map/reduce_scatter | solution.py:102
  295.4 1.0 add_convert_fusion
  296.5 26.0 %all_to_all.5 = bf16[16,16,512]{2,1,0:T(8,128)(2,1)S(1)} all-to-all(bf16[16,16,512]{2,1,0:T(8,128)(2,1)S(1)} %bitcast.87), channel_id=1, replica_groups=mesh['segment'=4,'seq'=16,'mp'=8] {'seq'}, dimensions={0} | all-to-all | bytes 524288 | tf_op jit(solution)/shard_map/all_to_all | solution.py:52
  322.5 4.8 %collective-permute-start.7 = (bf16[16,16,512]{2,1,0:T(8,128)(2,1)S(1)}, bf16[16,16,512]{2,1,0:T(8,128)(2,1)S(1)}, u32[]{:S(2)}, u32[]{:S(2)}) collective-permute-start(bf16[16,16,512]{2,1,0:T(8,128)(2,1)S(1)} %all_to_all.5), channel_id=1, source_target_pairs={{0,128},{128,256},{256,384},{384,0},{1,129},{129,257},{257,385},{3... | collective-permute-start | bytes 786440 | tf_op jit(solution)/shard_map/ppermute | solution.py:30
  327.3 5.8 %collective-permute-done.7 = bf16[16,16,512]{2,1,0:T(8,128)(2,1)S(1)} collective-permute-done((bf16[16,16,512]{2,1,0:T(8,128)(2,1)S(1)}, bf16[16,16,512]{2,1,0:T(8,128)(2,1)S(1)}, u32[]{:S(2)}, u32[]{:S(2)}) %collective-permute-start.7) | collective-permute-done | bytes 262176 | tf_op jit(solution)/shard_map/ppermute | solution.py:30
  333.1 0.7 copy.40
  (41 shorter events, 5.2 us)
Async XLA Ops:
  6.5 252.6 %copy-start = (f32[1,4096]{1,0:T(1,128)S(1)}, f32[1,4096]{1,0:T(1,128)}, u32[]{:S(2)}) copy-start(f32[1,4096]{1,0:T(1,128)} %param.14) | copy-start | bytes 49156
  6.5 3.2 copy-start.1
  6.5 164.9 %all-gather.3.cloned.1.call-start = ((), (), s32[]{:S(2)}) async-start(), calls=%async_computation.2 | async-start | bytes 13369344 | tf_op jit(solution)/shard_map/all_gather | solution.py:74
  8.9 245.4 %all-gather.5.cloned.1.call-start = ((), (), s32[]{:S(2)}) async-start(), calls=%async_computation.3 | async-start | bytes 4456448 | tf_op jit(solution)/shard_map/all_gather | solution.py:99
  9.7 285.8 %reduce-scatter.2.cloned.1.call-start = ((), (), s32[]{:S(2)}) async-start(), calls=%async_computation.4 | async-start | bytes 2359296 | tf_op jit(solution)/shard_map/reduce_scatter | solution.py:102
  9.7 9.7 %collective-permute-start = (bf16[1,1,256,512]{3,2,1,0:T(8,128)(2,1)S(1)}, bf16[1,1,256,512]{3,2,1,0:T(8,128)(2,1)S(1)}, u32[]{:S(2)}, u32[]{:S(2)}) collective-permute-start(bf16[1,1,256,512]{3,2,1,0:T(8,128)(2,1)S(1)} %copy-done.1), channel_id=1, source_target_pairs={{0,1},{1,2},{2,3},{3,4},{4,5},{5,6},{6,7},{7,0},{8,9},{9,10},{10,1... | collective-permute-start | bytes 786440 | tf_op jit(solution)/shard_map/ppermute | solution.py:18
  13.7 8.2 %collective-permute-start.1 = (bf16[1,1,256,512]{3,2,1,0:T(8,128)(2,1)S(1)}, bf16[1,1,256,512]{3,2,1,0:T(8,128)(2,1)S(1)}, u32[]{:S(2)}, u32[]{:S(2)}) collective-permute-start(bf16[1,1,256,512]{3,2,1,0:T(8,128)(2,1)S(1)} %copy-done.1), channel_id=1, source_target_pairs={{0,7},{1,0},{2,1},{3,2},{4,3},{5,4},{6,5},{7,6},{8,15},{9,8},{10,9... | collective-permute-start | bytes 786440 | tf_op jit(solution)/shard_map/ppermute | solution.py:21
  19.4 9.1 %collective-permute-start.2 = (bf16[1,1,256,512]{3,2,1,0:T(8,128)(2,1)S(1)}, bf16[1,1,256,512]{3,2,1,0:T(8,128)(2,1)S(1)}, u32[]{:S(2)}, u32[]{:S(2)}) collective-permute-start(bf16[1,1,256,512]{3,2,1,0:T(8,128)(2,1)S(1)} %collective-permute-done), channel_id=1, source_target_pairs={{0,1},{1,2},{2,3},{3,4},{4,5},{5,6},{6,7},{7,0},{8,9},{9,10},{10,1... | collective-permute-start | bytes 786440 | tf_op jit(solution)/shard_map/ppermute | solution.py:18
  21.9 8.5 %collective-permute-start.3 = (bf16[1,1,256,512]{3,2,1,0:T(8,128)(2,1)S(1)}, bf16[1,1,256,512]{3,2,1,0:T(8,128)(2,1)S(1)}, u32[]{:S(2)}, u32[]{:S(2)}) collective-permute-start(bf16[1,1,256,512]{3,2,1,0:T(8,128)(2,1)S(1)} %collective-permute-done.1), channel_id=1, source_target_pairs={{0,7},{1,0},{2,1},{3,2},{4,3},{5,4},{6,5},{7,6},{8,15},{9,8},{10,9... | collective-permute-start | bytes 786440 | tf_op jit(solution)/shard_map/ppermute | solution.py:21
  28.4 9.6 %collective-permute-start.4 = (bf16[1,1,256,512]{3,2,1,0:T(8,128)(2,1)S(1)}, bf16[1,1,256,512]{3,2,1,0:T(8,128)(2,1)S(1)}, u32[]{:S(2)}, u32[]{:S(2)}) collective-permute-start(bf16[1,1,256,512]{3,2,1,0:T(8,128)(2,1)S(1)} %collective-permute-done.2), channel_id=1, source_target_pairs={{0,1},{1,2},{2,3},{3,4},{4,5},{5,6},{6,7},{7,0},{8,9},{9,10},{10,1... | collective-permute-start | bytes 786440 | tf_op jit(solution)/shard_map/ppermute | solution.py:18
  30.4 9.6 %collective-permute-start.5 = (bf16[1,1,256,512]{3,2,1,0:T(8,128)(2,1)S(1)}, bf16[1,1,256,512]{3,2,1,0:T(8,128)(2,1)S(1)}, u32[]{:S(2)}, u32[]{:S(2)}) collective-permute-start(bf16[1,1,256,512]{3,2,1,0:T(8,128)(2,1)S(1)} %collective-permute-done.3), channel_id=1, source_target_pairs={{0,7},{1,0},{2,1},{3,2},{4,3},{5,4},{6,5},{7,6},{8,15},{9,8},{10,9... | collective-permute-start | bytes 786440 | tf_op jit(solution)/shard_map/ppermute | solution.py:21
  38.0 10.3 %collective-permute-start.6 = (bf16[1,1,256,512]{3,2,1,0:T(8,128)(2,1)S(1)}, bf16[1,1,256,512]{3,2,1,0:T(8,128)(2,1)S(1)}, u32[]{:S(2)}, u32[]{:S(2)}) collective-permute-start(bf16[1,1,256,512]{3,2,1,0:T(8,128)(2,1)S(1)} %collective-permute-done.4), channel_id=1, source_target_pairs={{0,1},{1,2},{2,3},{3,4},{4,5},{5,6},{6,7},{7,0},{8,9},{9,10},{10,1... | collective-permute-start | bytes 786440 | tf_op jit(solution)/shard_map/ppermute | solution.py:18
  48.3 123.1 %copy-start.3 = (f32[1,4096]{1,0:T(1,128)S(1)}, f32[1,4096]{1,0:T(1,128)}, u32[]{:S(2)}) copy-start(f32[1,4096]{1,0:T(1,128)} %param.12) | copy-start | bytes 49156
  48.4 123.0 %copy-start.4 = (f32[1,4096]{1,0:T(1,128)S(1)}, f32[1,4096]{1,0:T(1,128)}, u32[]{:S(2)}) copy-start(f32[1,4096]{1,0:T(1,128)} %param.13) | copy-start | bytes 49156
  171.4 8.1 %copy-start.2 = (s32[1,16]{1,0:T(1,128)S(1)}, s32[1,16]{1,0:T(1,128)}, u32[]{:S(2)}) copy-start(s32[1,16]{1,0:T(1,128)} %param.15) | copy-start | bytes 196
  322.5 10.6 %collective-permute-start.7 = (bf16[16,16,512]{2,1,0:T(8,128)(2,1)S(1)}, bf16[16,16,512]{2,1,0:T(8,128)(2,1)S(1)}, u32[]{:S(2)}, u32[]{:S(2)}) collective-permute-start(bf16[16,16,512]{2,1,0:T(8,128)(2,1)S(1)} %all_to_all.5), channel_id=1, source_target_pairs={{0,128},{128,256},{256,384},{384,0},{1,129},{129,257},{257,385},{3... | collective-permute-start | bytes 786440 | tf_op jit(solution)/shard_map/ppermute | solution.py:30
Sparse Core Ops, SparseCore 0:
  10.5 160.8 all-gather.2
  174.5 79.7 all-gather.4
  259.2 36.1 reduce-scatter.1
